TPU v7x, 32 devices: a whole 2x2x4 slice. The times are simulated.
32 devices in a mesh: groups: 2 (over y), frame: 4 (over x, core), row: 4 (over z).
Axes of the slice: x: 2, y: 2, z: 4, core: 2. Of those that a mesh axis runs over, the one named last changes fastest.
Arguments:
- query_in: bfloat16 [8, 4, 64, 2240], P(('groups', 'frame'), 'row'), parts along dimension 0, may hold values from -6 to 6
- key_in: bfloat16 [8, 4, 64, 2240], P(('groups', 'frame'), 'row'), parts along dimension 0, may hold values from -216 to 216
- value_in: bfloat16 [8, 4, 64, 2240], P(('groups', 'frame'), 'row'), parts along dimension 0, may hold values from -6 to 6
- stream_in: bfloat16 [8, 4, 64, 2240], P(('groups', 'frame'), 'row'), parts along dimension 0, may hold values from -6 to 6
- attn_gain: bfloat16 [2240], replicated, may hold values from 0.5 to 1.5
- ffn_gain: bfloat16 [2240], replicated, may hold values from 0.5 to 1.5
- in_weight: bfloat16 [2240, 2, 3360], P('row', None, 'frame'), may hold values from -0.125 to 0.125
- conv_weight: bfloat16 [9, 2, 3360], P(None, None, 'frame'), may hold values from -3.5 to 3.5
- out_weight: bfloat16 [3360, 2240], P('frame'), may hold values from -0.109375 to 0.109375
Outputs:
- stream_out: bfloat16 [8, 4, 64, 2240], P(('groups', 'frame'), 'row'), parts along dimension 0
- block_out: bfloat16 [8, 4, 64, 2240], P(('groups', 'frame'), 'row'), parts along dimension 0
There are 2 independent parts, one for each index of `groups`. A program takes and returns all parts, laid end to end along the dimension named above; an argument that names none is the same for every part. Nothing has to cross between parts.
All inputs are finite; a program needn't handle non-finite values.
Results may differ from a plain program's by a relative error of at most 0.01.
Values may be sent and summed in bfloat16 or wider, within the bound.
No kernel may reach another device: no remote copies, remote signals or barrier semaphores. Data moves between devices by JAX's collectives and lax.ppermute only.
A program may use at most 64 MiB of HBM per device.

v0:
```python
import jax
import jax.numpy as jnp
from jax import lax
from jax.sharding import PartitionSpec as P

HEADS = 20
HEAD_DIM = 112
NORM_EPS = 1e-06
SHARE_EPS = 1e-06


def padded_2(cells, sides, width):
    for axis, dim in sides:
        count = lax.axis_size(axis)
        ends = count - 1
        head = lax.slice_in_dim(cells, 0, width, axis=dim)
        tail = lax.slice_in_dim(cells, cells.shape[dim] - width, cells.shape[dim], axis=dim)
        cells = jnp.concatenate(
            [
                lax.ppermute(tail, axis, [(i, (i + 1) % count) for i in range(ends)]),
                cells,
                lax.ppermute(head, axis, [((i + 1) % count, i) for i in range(ends)]),
            ],
            axis=dim,
        )
    return cells


def rms_norm(features):
    return features * lax.rsqrt(jnp.mean(features * features, axis=-1, keepdims=True) + NORM_EPS)


def depthwise(padded, conv_taps, row_count, col_count, half_width):
    widened = jnp.pad(padded, ((0, 0), (0, 0), (1, 1), (0, 0)))
    summed = jnp.zeros((padded.shape[0], row_count, col_count, padded.shape[3]), jnp.float32)
    for row_off in range(3):
        for col_off in range(3):
            window = widened[
                :, row_off : row_off + row_count, col_off : col_off + col_count, :
            ].astype(jnp.float32)
            summed = summed + window * conv_taps[row_off * 3 + col_off]
    return (summed[..., :half_width] * jax.nn.silu(summed[..., half_width:])).astype(jnp.bfloat16)


def local(
    query_in, key_in, value_in, stream_in, attn_gain, ffn_gain, in_weight, conv_weight, out_weight
):
    frame_count, row_count, col_count, model_width = query_in.shape
    token_count = frame_count * row_count * col_count
    local_gated = in_weight.shape[2]
    highest = lax.Precision.HIGHEST
    key_pos = jnp.maximum(key_in, 0).reshape(token_count, HEADS, HEAD_DIM)
    value_heads = value_in.reshape(token_count, HEADS, HEAD_DIM)
    local_state = jnp.einsum(
        "thi,thj->ihj", key_pos, value_heads, preferred_element_type=jnp.float32
    ).reshape(HEAD_DIM, model_width)
    local_total = jnp.sum(key_pos.reshape(token_count, model_width), axis=0, dtype=jnp.float32)
    state_share, total_share = (
        lax.psum_scatter(
            local_state.astype(jnp.bfloat16), "row", scatter_dimension=1, tiled=True
        ).astype(jnp.float32),
        lax.psum_scatter(
            local_total.astype(jnp.bfloat16), "row", scatter_dimension=0, tiled=True
        ).astype(jnp.float32),
    )
    state_share, total_share = lax.psum((state_share, total_share), "frame")
    kv_state, key_total = (
        lax.all_gather(state_share, "row", axis=1, tiled=True),
        lax.all_gather(total_share, "row", axis=0, tiled=True),
    )
    query_pos = jnp.maximum(query_in, 0).reshape(token_count, HEADS, HEAD_DIM).astype(jnp.float32)
    numerator = jnp.einsum(
        "thi,ihj->thj", query_pos, kv_state.reshape(HEAD_DIM, HEADS, HEAD_DIM), precision=highest
    )
    denominator = jnp.einsum(
        "thi,hi->th", query_pos, key_total.reshape(HEADS, HEAD_DIM), precision=highest
    )
    attended = (numerator / (denominator[:, :, None] + SHARE_EPS)).reshape(token_count, model_width)
    stream_flat = stream_in.reshape(token_count, model_width).astype(jnp.float32)
    stream_out = (stream_flat + attn_gain.astype(jnp.float32) * rms_norm(attended)).astype(
        jnp.bfloat16
    )
    normed = (rms_norm(stream_out.astype(jnp.float32)) * ffn_gain.astype(jnp.float32)).astype(
        jnp.bfloat16
    )
    normed_grid = normed.reshape(frame_count, row_count, col_count, model_width)
    in_full = lax.all_gather(in_weight, "row", axis=0, tiled=True).reshape(
        model_width, 2 * local_gated
    )
    conv_taps = conv_weight.reshape(9, 2 * local_gated).astype(jnp.float32)
    frame_piece = lax.all_gather(normed_grid, "frame", axis=0, tiled=True)
    piece_frames = frame_piece.shape[0]
    piece_rows = frame_piece.shape[1]
    projected = jnp.dot(
        frame_piece.reshape(piece_frames * piece_rows * col_count, model_width),
        in_full,
        preferred_element_type=jnp.float32,
    )
    expanded = (
        jax.nn.silu(projected)
        .astype(jnp.bfloat16)
        .reshape(piece_frames, piece_rows, col_count, 2 * local_gated)
    )
    padded_expanded = padded_2(expanded, (("row", 1),), 1)
    hidden = depthwise(padded_expanded, conv_taps, row_count, col_count, local_gated)
    hidden_flat = hidden.reshape(-1, local_gated)
    ffn_rows = lax.psum_scatter(
        jnp.dot(hidden_flat, out_weight, preferred_element_type=jnp.float32).astype(jnp.bfloat16),
        "frame",
        scatter_dimension=0,
        tiled=True,
    ).astype(jnp.float32)
    block_out = (stream_out.astype(jnp.float32) + ffn_rows).astype(jnp.bfloat16)
    grid_shape = (frame_count, row_count, col_count, model_width)
    return (stream_out.reshape(grid_shape), block_out.reshape(grid_shape))


def solution(mesh):
    in_specs = (
        P(("groups", "frame"), "row", None, None),
        P(("groups", "frame"), "row", None, None),
        P(("groups", "frame"), "row", None, None),
        P(("groups", "frame"), "row", None, None),
        P(),
        P(),
        P("row", None, "frame"),
        P(None, None, "frame"),
        P("frame", None),
    )
    out_specs = (
        P(("groups", "frame"), "row", None, None),
        P(("groups", "frame"), "row", None, None),
    )
    return jax.shard_map(local, mesh=mesh, in_specs=in_specs, out_specs=out_specs, check_vma=False)
```

profile of v0, /device:TPU:0, one launch (start us, length us, event | category | flops | bytes accessed | tf_op | source)
XLA Modules:
  0.0 293.6 jit_solution(11495132540162727477)
XLA Ops:
  7.2 1.1 fusion.21
  8.3 0.4 reshape.204
  8.7 1.4 reshape.205
  10.1 0.4 fusion.7
  10.5 1.1 copy.25
  11.6 0.7 all-gather.5.cloned.1.call-update
  12.5 0.4 reshape.207
  12.9 0.6 fusion.25
  14.8 14.3 %all-reduce.2 = bf16[2240]{0:T(1024)(128)(2,1)S(1)} all-reduce(bf16[2240]{0:T(1024)(128)(2,1)S(1)} %get-tuple-element.8), channel_id=3, replica_groups=mesh['groups'=2,'frame'=4,'row'=4] {'row'}, use_global_device_ids=true, to_apply=%region_3.0.clone | all-reduce | flops 2240 | bytes 8960
  29.2 0.1 dynamic-slice_convert_fusion
  29.3 7.2 %reduce-scatter.3.cloned.1.call-done = bf16[112,560]{0,1:T(8,128)(2,1)} async-done(((bf16[112,2240]{0,1:T(8,128)(2,1)}), bf16[112,560]{0,1:T(8,128)(2,1)}) %reduce-scatter.3.cloned.1.call-update) | async-done | bytes 125456 | tf_op jit(solution)/shard_map/reduce_scatter | solution.py:59
  36.5 13.6 %all-reduce.5 = (f32[112,560]{0,1:T(8,128)S(1)}, f32[560]{0:T(1024)S(1)}) all-reduce(bf16[112,560]{0,1:T(8,128)(2,1)} %reduce-scatter.3.cloned.1.call-done, f32[560]{0:T(1024)S(1)} %dynamic-slice_convert_fusion), channel_id=1, replica_groups=mesh['groups'=2,'frame'=4,'row'=4] {'frame'}, use_global_device_ids=true, to_apply=%region_1.0 | all-reduce | flops 63280 | bytes 380800 | tf_op jit(solution)/shard_map/psum | solution.py:66
  50.1 0.3 dynamic-update-slice
  50.4 19.7 %all-reduce.1 = f32[2240]{0:T(1024)S(1)} all-reduce(f32[2240]{0:T(1024)S(1)} %dynamic-update-slice), channel_id=1, replica_groups=mesh['groups'=2,'frame'=4,'row'=4] {'row'}, use_global_device_ids=true, to_apply=%add.1 | all-reduce | flops 2240 | bytes 17920
  70.1 0.1 reshape.225
  70.2 0.6 fusion.17
  70.8 42.0 %all_gather.12 = f32[112,2240]{0,1:T(8,128)S(1)} all-gather(f32[112,560]{0,1:T(8,128)S(1)} %get-tuple-element.2), channel_id=1, replica_groups=mesh['groups'=2,'frame'=4,'row'=4] {'row'}, dimensions={1}, use_global_device_ids=true | all-gather | bytes 1254400 | tf_op jit(solution)/shard_map/all_gather | solution.py:68
  112.8 1.4 multiply_reduce_fusion
  114.2 0.4 copy.28
  114.6 0.2 reshape.210
  114.8 0.2 reshape.209
  115.1 0.1 copy-done
  115.1 0.3 fusion.12
  115.4 1.0 multiply_convert_fusion.1
  116.5 0.0 reduce-scatter.5.cloned.1.call-start
  116.6 82.5 %all-gather.5.cloned.1.call-done = bf16[2240,2,840]{2,1,0:T(2,128)(2,1)} async-done(((bf16[560,2,840]{2,1,0:T(2,128)(2,1)}), bf16[2240,2,840]{2,1,0:T(2,128)(2,1)}) %all-gather.5.cloned.1.call-update) | async-done | bytes 7526416 | tf_op jit(solution)/shard_map/all_gather | solution.py:87
  199.1 22.9 %copy.30 = bf16[2240,2,840]{0,2,1:T(8,128)(2,1)} copy(bf16[2240,2,840]{2,1,0:T(2,128)(2,1)} %all-gather.5.cloned.1.call-done) | data formatting | bytes 15052800 | tf_op jit(solution)/shard_map/all_gather | solution.py:87
  221.9 5.8 %multiply_convert_fusion = bf16[256,1680]{0,1:T(8,128)(2,1)S(1)} fusion(bf16[256,2240]{1,0:T(8,128)(2,1)} %bitcast.49, bf16[2240,1680]{0,1:T(8,128)(2,1)} %bitcast.45), kind=kOutput, calls=%fused_computation.10 | convolution fusion | flops 1928908800 | bytes 9533440 | tf_op jit(solution)/shard_map/dot_general | solution.py:94
  227.8 0.6 copy.31
  228.4 1.3 collective-permute-start.1
  229.7 4.8 %collective-permute-start = (bf16[4,1,64,1680]{3,2,0,1:T(8,128)(2,1)S(1)}, bf16[4,1,64,1680]{3,2,0,1:T(8,128)(2,1)S(1)}, u32[]{:S(2)}, u32[]{:S(2)}) collective-permute-start(bf16[4,1,64,1680]{3,2,0,1:T(8,128)(2,1)S(1)} %bitcast.42), channel_id=1, source_target_pairs={{0,1},{1,2},{2,3},{4,5},{5,6},{6,7},{8,9},{9,10},{10,11},{12,13},{... | collective-permute-start | bytes 2580488 | tf_op jit(solution)/shard_map/ppermute | solution.py:20
  234.5 0.1 mul.187
  234.6 0.1 mul.190
  234.7 0.1 mul.193
  234.8 0.1 mul.196
  234.8 0.1 mul.199
  234.9 0.1 mul.202
  235.0 0.1 mul.205
  235.1 0.1 mul.208
  235.2 0.1 mul.211
  235.2 17.3 %collective-permute-done.1 = bf16[4,1,64,1680]{3,2,0,1:T(8,128)(2,1)S(1)} collective-permute-done((bf16[4,1,64,1680]{3,2,0,1:T(8,128)(2,1)S(1)}, bf16[4,1,64,1680]{3,2,0,1:T(8,128)(2,1)S(1)}, u32[]{:S(2)}, u32[]{:S(2)}) %collective-permute-start.1) | collective-permute-done | bytes 860192 | tf_op jit(solution)/shard_map/ppermute | solution.py:22
  252.6 1.2 collective-permute-done
  253.8 1.1 fusion.5
  254.9 1.8 multiply_add_fusion
  256.6 0.3 fusion.8
  257.0 2.4 convolution_convert_fusion
  259.4 26.0 %reduce-scatter.5.cloned.1.call-done = bf16[64,2240]{1,0:T(8,128)(2,1)} async-done(((bf16[256,2240]{1,0:T(8,128)(2,1)}), bf16[64,2240]{1,0:T(8,128)(2,1)}) %reduce-scatter.5.cloned.1.call-update) | async-done | bytes 286736 | tf_op jit(solution)/shard_map/reduce_scatter | solution.py:107
  285.4 1.7 fusion.16
  (28 shorter events, 0.3 us)
Async XLA Ops:
  7.2 29.3 %reduce-scatter.3.cloned.1.call-start = ((), (), s32[]{:S(2)}) async-start(), calls=%async_computation.2 | async-start | bytes 716800 | tf_op jit(solution)/shard_map/reduce_scatter | solution.py:59
  10.4 2.0 copy-start.3
  10.5 2.0 copy-start.4
  10.5 2.0 copy-start.1
  11.6 1.4 copy-start.5
  11.6 187.5 %all-gather.5.cloned.1.call-start = ((), (), s32[]{:S(2)}) async-start(), calls=%async_computation.4 | async-start | bytes 10035200 | tf_op jit(solution)/shard_map/all_gather | solution.py:87
  12.4 209.6 %all-gather.3.cloned.1.call-start = ((), (), s32[]{:S(2)}) async-start(), calls=%async_computation.3 | async-start | bytes 1474560 | tf_op jit(solution)/shard_map/all_gather | solution.py:91
  114.2 1.0 copy-start
  116.5 168.9 %reduce-scatter.5.cloned.1.call-start = ((), (), s32[]{:S(2)}) async-start(), calls=%async_computation.5 | async-start | bytes 1474560 | tf_op jit(solution)/shard_map/reduce_scatter | solution.py:107
  221.9 12.6 %copy-start.2 = (bf16[9,2,840]{2,1,0:T(2,128)(2,1)S(1)}, bf16[9,2,840]{2,1,0:T(2,128)(2,1)}, u32[]{:S(2)}) copy-start(bf16[9,2,840]{2,1,0:T(2,128)(2,1)} %param.16) | copy-start | bytes 90724
  228.4 24.2 %collective-permute-start.1 = (bf16[4,1,64,1680]{3,2,0,1:T(8,128)(2,1)S(1)}, bf16[4,1,64,1680]{3,2,0,1:T(8,128)(2,1)S(1)}, u32[]{:S(2)}, u32[]{:S(2)}) collective-permute-start(bf16[4,1,64,1680]{3,2,0,1:T(8,128)(2,1)S(1)} %bitcast.41), channel_id=1, source_target_pairs={{1,0},{2,1},{3,2},{5,4},{6,5},{7,6},{9,8},{10,9},{11,10},{13,12},{... | collective-permute-start | bytes 2580488 | tf_op jit(solution)/shard_map/ppermute | solution.py:22
  229.7 24.1 %collective-permute-start = (bf16[4,1,64,1680]{3,2,0,1:T(8,128)(2,1)S(1)}, bf16[4,1,64,1680]{3,2,0,1:T(8,128)(2,1)S(1)}, u32[]{:S(2)}, u32[]{:S(2)}) collective-permute-start(bf16[4,1,64,1680]{3,2,0,1:T(8,128)(2,1)S(1)} %bitcast.42), channel_id=1, source_target_pairs={{0,1},{1,2},{2,3},{4,5},{5,6},{6,7},{8,9},{9,10},{10,11},{12,13},{... | collective-permute-start | bytes 2580488 | tf_op jit(solution)/shard_map/ppermute | solution.py:20
  254.8 2.1 copy-start.6
Sparse Core Ops, SparseCore 0:
  11.7 24.6 reduce-scatter.2
  38.0 160.9 all-gather.4
  201.2 15.6 all-gather.2
  259.5 25.7 reduce-scatter.4
where the time goes:
time: 295 us; the launch traced here: 294 us
  waiting for transfers between devices  135 us (46%)
  blocking collectives  89.6 us (30%)
  local copies, waits for them, and re-layouts  29.5 us (10%)
  between operations  15.4 us (5%)
  matrix products  10.6 us (4%)
  other arithmetic  7.42 us (3%)
  starting transfers between devices  6.24 us (2%)
    all_gather x1, waiting for transfers between devices, local(): lax.all_gather(in_weight, 'row', axis=0, tiled=True)  82.5 us
    all_gather x1, blocking collectives, local(): lax.all_gather(state_share, 'row', axis=1, tiled=True)  42 us
    unnamed x2, blocking collectives  34 us
    reduce_scatter x1, waiting for transfers between devices, local(): lax.psum_scatter(jnp.dot(hidden_flat, out_weight, preferred_element_type=...  26 us
    all_gather x1, local copies, waits for them, and re-layouts, local(): lax.all_gather(in_weight, 'row', axis=0, tiled=True)  22.9 us
    ppermute x1, waiting for transfers between devices, padded_2(): lax.ppermute(head, axis, [((i + 1) % count, i) for i in range(ends)])  17.3 us
    psum x1, blocking collectives, local(): state_share, total_share = lax.psum((state_share, total_share), 'frame')  13.6 us
    reduce_scatter x1, waiting for transfers between devices, local(): lax.psum_scatter(local_state.astype(jnp.bfloat16), 'row', scatter_dimensi...  7.19 us
  transfers between devices with their start and end apart: 6, of which 5 were waited for; matrix products, arithmetic and copies ran while one was open for 10% of the time, Pallas kernels for 0%

commit v1 on v0

--- a/solution.py
+++ b/solution.py
@@ -7,6 +7,27 @@
 HEAD_DIM = 112
 NORM_EPS = 1e-06
 SHARE_EPS = 1e-06
+
+
+def laid_out(tiles, dim):
+    lengths = list(tiles.shape[1:])
+    lengths[dim] *= tiles.shape[0]
+    return jnp.moveaxis(tiles, 0, dim).reshape(lengths)
+
+
+def collected_by_bits(x, axis):
+    peers, position = (lax.axis_size(axis), lax.axis_index(axis))
+    blocks, bit = (x[None], 1)
+    while bit < peers:
+        other = lax.ppermute(blocks, axis, [(i, i ^ bit) for i in range(peers)])
+        low = position & bit == 0
+        blocks = jnp.concatenate([jnp.where(low, blocks, other), jnp.where(low, other, blocks)])
+        bit *= 2
+    return blocks
+
+
+def doubled_up(x, axis, dim):
+    return laid_out(collected_by_bits(x, axis), dim)
 
 
 def padded_2(cells, sides, width):
@@ -84,9 +105,7 @@
         jnp.bfloat16
     )
     normed_grid = normed.reshape(frame_count, row_count, col_count, model_width)
-    in_full = lax.all_gather(in_weight, "row", axis=0, tiled=True).reshape(
-        model_width, 2 * local_gated
-    )
+    in_full = doubled_up(in_weight, "row", 0).reshape(model_width, 2 * local_gated)
     conv_taps = conv_weight.reshape(9, 2 * local_gated).astype(jnp.float32)
     frame_piece = lax.all_gather(normed_grid, "frame", axis=0, tiled=True)
     piece_frames = frame_piece.shape[0]

time: 295 us -> 425 us (1.44)
  blocking collectives: 89.6 us -> 231 us
  waiting for transfers between devices: 135 us -> 81.3 us
  other arithmetic: 7.42 us -> 47.6 us
  starting transfers between devices: 6.24 us -> 12.3 us
  local copies, waits for them, and re-layouts: 29.5 us -> 24.2 us
    unnamed x2, blocking collectives: 34 us -> 195 us
    all_gather x1 -> x0, waiting for transfers between devices: 82.5 us -> none  [local(): lax.all_gather(in_weight, 'row', axis=0, tiled=True)]
    ppermute x0 -> x2, waiting for transfers between devices: none -> 41.2 us  [collected_by_bits(): other = lax.ppermute(blocks, axis, [(i, i ^ bit) for i in range(peers)])]
    all_gather x1 -> x0, local copies, waits for them, and re-layouts: 22.9 us -> none  [local(): lax.all_gather(in_weight, 'row', axis=0, tiled=True)]
    all_gather x1, blocking collectives: 42 us -> 20.4 us  [local(): lax.all_gather(state_share, 'row', axis=1, tiled=True)]
    concatenate x0 -> x2, other arithmetic: none -> 19.7 us  [collected_by_bits(): jnp.concatenate([jnp.where(low, blocks, other), jnp.where(low, other, blo...]
    another operation x0 -> x1, local copies, waits for them, and re-layouts: none -> 16.9 us  [local(): doubled_up(in_weight, 'row', 0).reshape(model_width, 2 * local_gated)]
    select_n x0 -> x2, other arithmetic: none -> 16.6 us  [collected_by_bits(): jnp.where(low, blocks, other)]
  transfers between devices with their start and end apart: 6 -> 7, of which waited for: 5 -> 5; matrix products, arithmetic and copies ran while one was open for 10% -> 13% of each run, Pallas kernels for 0% -> 0%
where the time goes in v1:
time: 425 us; the launch traced here: 424 us
  blocking collectives  231 us (54%)
  waiting for transfers between devices  81.3 us (19%)
  other arithmetic  47.6 us (11%)
  local copies, waits for them, and re-layouts  24.2 us (6%)
  between operations  15.3 us (4%)
  starting transfers between devices  12.3 us (3%)
  matrix products  11.7 us (3%)
    unnamed x2, blocking collectives  195 us
    ppermute x2, waiting for transfers between devices, collected_by_bits(): other = lax.ppermute(blocks, axis, [(i, i ^ bit) for i in range(peers)])  41.2 us
    reduce_scatter x1, waiting for transfers between devices, local(): lax.psum_scatter(jnp.dot(hidden_flat, out_weight, preferred_element_type=...  26.4 us
    all_gather x1, blocking collectives, local(): lax.all_gather(state_share, 'row', axis=1, tiled=True)  20.4 us
    concatenate x2, other arithmetic, collected_by_bits(): jnp.concatenate([jnp.where(low, blocks, other), jnp.where(low, other, blo...  19.7 us
    another operation x1, local copies, waits for them, and re-layouts, local(): doubled_up(in_weight, 'row', 0).reshape(model_width, 2 * local_gated)  16.9 us
    select_n x2, other arithmetic, collected_by_bits(): jnp.where(low, blocks, other)  16.6 us
    psum x1, blocking collectives, local(): state_share, total_share = lax.psum((state_share, total_share), 'frame')  15.6 us
  transfers between devices with their start and end apart: 7, of which 5 were waited for; matrix products, arithmetic and copies ran while one was open for 13% of the time, Pallas kernels for 0%

profile of v1, /device:TPU:0, one launch (start us, length us, event | category | flops | bytes accessed | tf_op | source)
XLA Modules:
  0.0 423.7 jit_solution(3902322712551202025)
XLA Ops:
  7.2 3.1 collective-permute-start
  10.3 1.4 reshape.202
  11.7 1.1 fusion.21
  12.7 0.4 reshape.201
  13.2 41.2 %collective-permute-done = bf16[1,560,2,840]{3,2,1,0:T(2,128)(2,1)} collective-permute-done((bf16[1,560,2,840]{3,2,1,0:T(2,128)(2,1)}, bf16[1,560,2,840]{3,2,1,0:T(2,128)(2,1)}, u32[]{:S(2)}, u32[]{:S(2)}) %collective-permute-start) | collective-permute-done | bytes 1881632 | tf_op jit(solution)/shard_map/ppermute | solution.py:22
  54.3 5.5 %broadcast_select_fusion.3 = (bf16[1,560,2,840]{3,2,1,0:T(2,128)(2,1)S(1)}, bf16[1,560,2,840]{3,2,1,0:T(2,128)(2,1)S(1)}) fusion(bf16[1,560,2,840]{3,2,1,0:T(2,128)(2,1)} %collective-permute-done, pred[]{:T(512)S(6)} %eq.7, bf16[560,2,840]{2,1,0:T(2,128)(2,1)} %param.15), kind=kLoop, calls=%fused_computation.8 | loop fusion | flops 1881600 | bytes 7526401 | tf_op jit(solution)/shard_map/jit(_where)/select_n | solution.py:24
  59.9 7.8 %pad_maximum_fusion.1 = bf16[2,560,2,840]{3,2,1,0:T(2,128)(2,1)} fusion(bf16[1,560,2,840]{3,2,1,0:T(2,128)(2,1)S(1)} %get-tuple-element.11, bf16[1,560,2,840]{3,2,1,0:T(2,128)(2,1)S(1)} %get-tuple-element.10), kind=kLoop, calls=%fused_computation.6 | loop fusion | flops 1881600 | bytes 7526400 | tf_op jit(solution)/shard_map/concatenate | solution.py:24
  67.7 2.8 collective-permute-start.1
  70.5 0.4 fusion.7
  70.9 1.0 copy.24
  72.0 0.2 all-gather.2.cloned.1.call-start
  72.2 1.0 broadcast_maximum_fusion
  73.2 0.4 reshape.204
  73.7 0.6 fusion.25
  75.6 96.3 %all-reduce.2 = bf16[2240]{0:T(1024)(128)(2,1)S(1)} all-reduce(bf16[2240]{0:T(1024)(128)(2,1)S(1)} %get-tuple-element.12), channel_id=3, replica_groups=mesh['groups'=2,'frame'=4,'row'=4] {'row'}, use_global_device_ids=true, to_apply=%region_3.0.clone | all-reduce | flops 2240 | bytes 8960
  171.8 0.1 dynamic-slice_convert_fusion
  171.9 0.9 reduce-scatter.3.cloned.1.call-done
  172.9 15.6 %all-reduce.5 = (f32[112,560]{0,1:T(8,128)S(1)}, f32[560]{0:T(1024)S(1)}) all-reduce(bf16[112,560]{0,1:T(8,128)(2,1)} %reduce-scatter.3.cloned.1.call-done, f32[560]{0:T(1024)S(1)} %dynamic-slice_convert_fusion), channel_id=1, replica_groups=mesh['groups'=2,'frame'=4,'row'=4] {'frame'}, use_global_device_ids=true, to_apply=%region_1.0 | all-reduce | flops 63280 | bytes 380800 | tf_op jit(solution)/shard_map/psum | solution.py:87
  188.4 0.3 dynamic-update-slice
  188.7 99.1 %all-reduce.1 = f32[2240]{0:T(1024)S(1)} all-reduce(f32[2240]{0:T(1024)S(1)} %dynamic-update-slice), channel_id=1, replica_groups=mesh['groups'=2,'frame'=4,'row'=4] {'row'}, use_global_device_ids=true, to_apply=%add.1 | all-reduce | flops 2240 | bytes 17920
  287.9 0.1 reshape.221
  287.9 0.6 fusion.17
  288.6 20.4 %all_gather.9 = f32[112,2240]{0,1:T(8,128)S(1)} all-gather(f32[112,560]{0,1:T(8,128)S(1)} %get-tuple-element.2), channel_id=1, replica_groups=mesh['groups'=2,'frame'=4,'row'=4] {'row'}, dimensions={1}, use_global_device_ids=true | all-gather | bytes 1254400 | tf_op jit(solution)/shard_map/all_gather | solution.py:89
  309.0 1.4 multiply_reduce_fusion
  310.4 0.4 copy.27
  310.8 1.0 reshape.207
  311.8 0.2 reshape.206
  312.0 2.1 fusion.12
  314.2 2.0 multiply_convert_fusion.1
  316.3 11.1 %broadcast_select_fusion.1 = (bf16[2,560,2,840]{3,2,1,0:T(2,128)(2,1)S(1)}, bf16[2,560,2,840]{3,2,1,0:T(2,128)(2,1)S(1)}) fusion(bf16[2,560,2,840]{3,2,1,0:T(2,128)(2,1)} %collective-permute-done.1, pred[]{:T(512)S(6)} %eq.6, bf16[1,560,2,840]{3,2,1,0:T(2,128)(2,1)} %copy-done, bf16[1,560,2,840]{3,2,1,0:T(2,128)(2,1)S(1)} %get-tuple-element.10), kind=kLoop, calls=%fused_computation.4 | loop fusion | flops 5644800 | bytes 15052801 | tf_op jit(solution)/shard_map/jit(_where)/select_n | solution.py:24
  327.4 11.9 %pad_maximum_fusion = bf16[4,560,2,840]{3,2,1,0:T(2,128)(2,1)} fusion(bf16[2,560,2,840]{3,2,1,0:T(2,128)(2,1)S(1)} %get-tuple-element.9, bf16[2,560,2,840]{3,2,1,0:T(2,128)(2,1)S(1)} %get-tuple-element.8), kind=kLoop, calls=%fused_computation.2 | loop fusion | flops 3763200 | bytes 15052800 | tf_op jit(solution)/shard_map/concatenate | solution.py:24
  339.3 16.9 %reshape_reshape.4 = bf16[2240,1680]{1,0:T(8,128)(2,1)} reshape(bf16[4,560,2,840]{3,2,1,0:T(2,128)(2,1)} %pad_maximum_fusion) | data formatting | bytes 15052800 | tf_op jit(solution)/shard_map/reshape;reshape | solution.py:108
  356.2 6.9 %multiply_convert_fusion = bf16[256,1680]{0,1:T(8,128)(2,1)S(1)} fusion(bf16[256,2240]{1,0:T(8,128)(2,1)} %bitcast.51, bf16[2240,1680]{1,0:T(8,128)(2,1)} %reshape_reshape.4), kind=kOutput, calls=%fused_computation.16 | convolution fusion | flops 1928908800 | bytes 9533440 | tf_op jit(solution)/shard_map/dot_general | solution.py:113
  363.1 0.6 copy.29
  363.7 1.3 collective-permute-start.3
  365.0 4.8 %collective-permute-start.2 = (bf16[4,1,64,1680]{3,2,0,1:T(8,128)(2,1)S(1)}, bf16[4,1,64,1680]{3,2,0,1:T(8,128)(2,1)S(1)}, u32[]{:S(2)}, u32[]{:S(2)}) collective-permute-start(bf16[4,1,64,1680]{3,2,0,1:T(8,128)(2,1)S(1)} %bitcast.44), channel_id=1, source_target_pairs={{0,1},{1,2},{2,3},{4,5},{5,6},{6,7},{8,9},{9,10},{10,11},{12,13},{... | collective-permute-start | bytes 2580488 | tf_op jit(solution)/shard_map/ppermute | solution.py:41
  369.9 0.1 mul.211
  370.4 0.1 mul.193
  370.5 0.1 mul.190
  370.6 0.1 mul.187
  370.6 11.6 %collective-permute-done.3 = bf16[4,1,64,1680]{3,2,0,1:T(8,128)(2,1)S(1)} collective-permute-done((bf16[4,1,64,1680]{3,2,0,1:T(8,128)(2,1)S(1)}, bf16[4,1,64,1680]{3,2,0,1:T(8,128)(2,1)S(1)}, u32[]{:S(2)}, u32[]{:S(2)}) %collective-permute-start.3) | collective-permute-done | bytes 860192 | tf_op jit(solution)/shard_map/ppermute | solution.py:43
  382.2 1.2 collective-permute-done.2
  383.4 1.1 fusion.5
  384.5 1.8 multiply_add_fusion
  386.2 0.4 fusion.8
  386.6 2.4 convolution_convert_fusion
  389.1 26.4 %reduce-scatter.5.cloned.1.call-done = bf16[64,2240]{1,0:T(8,128)(2,1)} async-done(((bf16[256,2240]{1,0:T(8,128)(2,1)}), bf16[64,2240]{1,0:T(8,128)(2,1)}) %reduce-scatter.5.cloned.1.call-update) | async-done | bytes 286736 | tf_op jit(solution)/shard_map/reduce_scatter | solution.py:126
  415.5 1.7 fusion.16
  (33 shorter events, 0.6 us)
Async XLA Ops:
  7.2 165.7 %reduce-scatter.3.cloned.1.call-start = ((), (), s32[]{:S(2)}) async-start(), calls=%async_computation.2 | async-start | bytes 716800 | tf_op jit(solution)/shard_map/reduce_scatter | solution.py:80
  7.2 47.1 %collective-permute-start = (bf16[1,560,2,840]{3,2,1,0:T(2,128)(2,1)}, bf16[1,560,2,840]{3,2,1,0:T(2,128)(2,1)}, u32[]{:S(2)}, u32[]{:S(2)}) collective-permute-start(bf16[1,560,2,840]{3,2,1,0:T(2,128)(2,1)} %bitcast.48), channel_id=1, source_target_pairs={{0,1},{1,0},{2,3},{3,2},{4,5},{5,4},{6,7},{7,6},{8,9},{9,8},{10,11... | collective-permute-start | bytes 5644808 | tf_op jit(solution)/shard_map/ppermute | solution.py:22
  59.8 7.9 %copy-start = (bf16[1,560,2,840]{3,2,1,0:T(2,128)(2,1)}, bf16[1,560,2,840]{3,2,1,0:T(2,128)(2,1)S(1)}, u32[]{:S(2)}) copy-start(bf16[1,560,2,840]{3,2,1,0:T(2,128)(2,1)S(1)} %get-tuple-element.11) | copy-start | bytes 5644804
  67.7 4.5 %copy-start.3 = (bf16[2240]{0:T(1024)(128)(2,1)S(1)}, bf16[2240]{0:T(1024)(128)(2,1)}, u32[]{:S(2)}) copy-start(bf16[2240]{0:T(1024)(128)(2,1)} %param.14) | copy-start | bytes 13444
  67.7 5.9 %copy-start.4 = (bf16[2240]{0:T(1024)(128)(2,1)S(1)}, bf16[2240]{0:T(1024)(128)(2,1)}, u32[]{:S(2)}) copy-start(bf16[2240]{0:T(1024)(128)(2,1)} %param.13) | copy-start | bytes 13444
  67.7 6.0 %copy-start.5 = (u32[32]{0:T(128)S(1)}, u32[32]{0:T(128)}, u32[]{:S(2)}) copy-start(u32[32]{0:T(128)} %constant.36) | copy-start | bytes 388
  67.7 248.6 %collective-permute-start.1 = (bf16[2,560,2,840]{3,2,1,0:T(2,128)(2,1)}, bf16[2,560,2,840]{3,2,1,0:T(2,128)(2,1)}, u32[]{:S(2)}, u32[]{:S(2)}) collective-permute-start(bf16[2,560,2,840]{3,2,1,0:T(2,128)(2,1)} %pad_maximum_fusion.1), channel_id=1, source_target_pairs={{0,2},{1,3},{2,0},{3,1},{4,6},{5,7},{6,4},{7,5},{8,10},{9,11},{10,... | collective-permute-start | bytes 11289608 | tf_op jit(solution)/shard_map/ppermute | solution.py:22
  72.0 284.2 %all-gather.2.cloned.1.call-start = ((), (), s32[]{:S(2)}) async-start(), calls=%async_computation.3 | async-start | bytes 1474560 | tf_op jit(solution)/shard_map/all_gather | solution.py:110
  316.2 99.2 %reduce-scatter.5.cloned.1.call-start = ((), (), s32[]{:S(2)}) async-start(), calls=%async_computation.4 | async-start | bytes 1474560 | tf_op jit(solution)/shard_map/reduce_scatter | solution.py:126
  356.2 13.7 %copy-start.2 = (bf16[9,2,840]{2,1,0:T(2,128)(2,1)S(1)}, bf16[9,2,840]{2,1,0:T(2,128)(2,1)}, u32[]{:S(2)}) copy-start(bf16[9,2,840]{2,1,0:T(2,128)(2,1)} %param.16) | copy-start | bytes 90724
  363.7 18.4 %collective-permute-start.3 = (bf16[4,1,64,1680]{3,2,0,1:T(8,128)(2,1)S(1)}, bf16[4,1,64,1680]{3,2,0,1:T(8,128)(2,1)S(1)}, u32[]{:S(2)}, u32[]{:S(2)}) collective-permute-start(bf16[4,1,64,1680]{3,2,0,1:T(8,128)(2,1)S(1)} %bitcast.43), channel_id=1, source_target_pairs={{1,0},{2,1},{3,2},{5,4},{6,5},{7,6},{9,8},{10,9},{11,10},{13,12},{... | collective-permute-start | bytes 2580488 | tf_op jit(solution)/shard_map/ppermute | solution.py:43
  365.0 18.3 %collective-permute-start.2 = (bf16[4,1,64,1680]{3,2,0,1:T(8,128)(2,1)S(1)}, bf16[4,1,64,1680]{3,2,0,1:T(8,128)(2,1)S(1)}, u32[]{:S(2)}, u32[]{:S(2)}) collective-permute-start(bf16[4,1,64,1680]{3,2,0,1:T(8,128)(2,1)S(1)} %bitcast.44), channel_id=1, source_target_pairs={{0,1},{1,2},{2,3},{4,5},{5,6},{6,7},{8,9},{9,10},{10,11},{12,13},{... | collective-permute-start | bytes 2580488 | tf_op jit(solution)/shard_map/ppermute | solution.py:41
  384.4 2.2 copy-start.6
  386.6 28.9 %copy-start.1 = (bf16[64,2240]{1,0:T(8,128)(2,1)S(1)}, bf16[64,2240]{1,0:T(8,128)(2,1)}, u32[]{:S(2)}) copy-start(bf16[64,2240]{1,0:T(8,128)(2,1)} %get-tuple-element.7) | copy-start | bytes 860164
Sparse Core Ops, SparseCore 0:
  72.1 100.7 reduce-scatter.2
  316.3 16.5 all-gather.1
  389.2 26.2 reduce-scatter.4
